TPU v7x, 256 devices: a whole 4x4x8 slice. The times are simulated.
256 devices in a mesh: fsdp: 16 (over x, y), seq: 16 (over z, core).
Axes of the slice: x: 4, y: 4, z: 8, core: 2. Of those that a mesh axis runs over, the one named last changes fastest.
Arguments:
- tokens: bfloat16 [65536, 2048], P(('fsdp', 'seq')), may hold values from -6 to 6
- seq_lengths: int32 [16, 4], P('fsdp'), may hold values from 1 to 2048, 4096 in all within a row
- in_weight: bfloat16 [2048, 6144], P(None, 'fsdp'), may hold values from -0.125 to 0.125
- short_filter: float32 [7, 6144], replicated, may hold values from -2.5 to 2.5
- long_filter: bfloat16 [128, 128], replicated, may hold values from -0.5 to 0.5
- out_weight: bfloat16 [2048, 2048], replicated, may hold values from -0.125 to 0.125
Outputs:
- mixed: bfloat16 [65536, 2048], P(('fsdp', 'seq'))
Inputs may be any that keep to these rules, and one draw needn't show every extreme that they name: `seq_lengths`: in each pack the 4 lengths sum to 4096 and the longest is exactly 2048.
All inputs are finite; a program needn't handle non-finite values.
Results may differ from a plain program's by a relative error of at most 0.0073.
Values may be sent and summed in bfloat16 or wider, within the bound.
No kernel may reach another device: no remote copies, remote signals or barrier semaphores. Data moves between devices by JAX's collectives and lax.ppermute only.
A program may use at most 128 MiB of HBM per device.

v0:
```python
import jax
import jax.numpy as jnp
from jax import lax
from jax.sharding import PartitionSpec as P


def from_behind(block, axis, distance):
    devices = range(lax.axis_size(axis))
    route = [(i - distance, i) for i in devices if i - distance in devices]
    return lax.ppermute(block, axis, route)


def positions(row_ids, seq_starts):
    seq_begin = jnp.max(
        jnp.where(seq_starts[None, :] <= row_ids[:, None], seq_starts[None, :], 0), axis=1
    )
    return row_ids - seq_begin


def featurize(extended, position, taps):
    width = taps.shape[0]
    rows = position.shape[0]
    total = jnp.zeros((rows, extended.shape[1]), jnp.float32)
    for tap_index in range(width):
        part = extended[width - 1 - tap_index : width - 1 - tap_index + rows].astype(jnp.float32)
        total = total + taps[tap_index] * jnp.where((position >= tap_index)[:, None], part, 0.0)
    return total


def tap_table(tap_ids, long_filter):
    filter_len = long_filter.shape[0]
    one_hot = (
        tap_ids[:, :, None] == jnp.arange(filter_len, dtype=jnp.int32)[None, None, :]
    ).astype(jnp.bfloat16)
    return jnp.einsum(
        "ijt,tg->ijg", one_hot, long_filter, preferred_element_type=jnp.float32
    ).astype(jnp.bfloat16)


def local(tokens, seq_lengths, in_weight, short_filter, long_filter, out_weight):
    row_count, channels = tokens.shape
    width = short_filter.shape[0]
    filter_len, group_count = long_filter.shape
    projected = jnp.dot(
        tokens,
        lax.all_gather(in_weight, "fsdp", axis=1, tiled=True),
        preferred_element_type=jnp.float32,
    ).astype(jnp.bfloat16)
    lengths_row = seq_lengths[0]
    seq_starts = jnp.cumsum(lengths_row) - lengths_row
    first_global = lax.axis_index("seq") * row_count
    row_ids = first_global + jnp.arange(row_count, dtype=jnp.int32)
    position = positions(row_ids, seq_starts)
    prev_tail = from_behind(projected[row_count - (width - 1) :], "seq", 1)
    extended = jnp.concatenate([prev_tail, projected], axis=0)
    featured = featurize(extended, position, short_filter)
    queries = featured[:, :channels]
    mixed_in = (featured[:, channels : 2 * channels] * featured[:, 2 * channels :]).astype(
        jnp.bfloat16
    )
    conv_tail = from_behind(mixed_in[row_count - (filter_len - 1) :], "seq", 1)
    window_all = jnp.concatenate([conv_tail, mixed_in], axis=0)
    out_rows = jnp.arange(filter_len, dtype=jnp.int32)[:, None]
    cur_tap = out_rows - jnp.arange(filter_len, dtype=jnp.int32)[None, :]
    prev_tap = out_rows + (filter_len - 1) - jnp.arange(filter_len - 1, dtype=jnp.int32)[None, :]
    cur_table = tap_table(cur_tap, long_filter)
    prev_table = tap_table(prev_tap, long_filter)
    per_group = channels // group_count
    pieces = []
    for block_id in range(row_count // filter_len):
        first_row = block_id * filter_len
        block_pos = position[first_row : first_row + filter_len]
        cur_kernel = jnp.where((cur_tap <= block_pos[:, None])[:, :, None], cur_table, 0.0)
        prev_kernel = jnp.where((prev_tap <= block_pos[:, None])[:, :, None], prev_table, 0.0)
        prev_src = window_all[first_row : first_row + filter_len - 1].reshape(
            filter_len - 1, group_count, per_group
        )
        cur_src = window_all[first_row + filter_len - 1 : first_row + 2 * filter_len - 1].reshape(
            filter_len, group_count, per_group
        )
        block_out = jnp.einsum(
            "ijg,jgc->igc", cur_kernel, cur_src, preferred_element_type=jnp.float32
        )
        block_out = block_out + jnp.einsum(
            "ijg,jgc->igc", prev_kernel, prev_src, preferred_element_type=jnp.float32
        )
        pieces.append(block_out.reshape(filter_len, channels))
    filtered = jnp.concatenate(pieces, axis=0)
    gated_out = (queries * filtered).astype(jnp.bfloat16)
    result = tokens.astype(jnp.float32) + jnp.dot(
        gated_out, out_weight, preferred_element_type=jnp.float32
    )
    return result.astype(jnp.bfloat16)


def solution(mesh):
    in_specs = (P(("fsdp", "seq"), None), P("fsdp", None), P(None, "fsdp"), P(), P(), P())
    out_specs = P(("fsdp", "seq"), None)
    return jax.shard_map(local, mesh=mesh, in_specs=in_specs, out_specs=out_specs, check_vma=False)
```

profile of v0, /device:TPU:1, one launch (start us, length us, event | category | flops | bytes accessed | tf_op | source)
XLA Modules:
  0.0 275.3 jit_solution(17743482276146317237)
XLA Ops:
  6.5 0.7 all-gather.2.cloned.1.call-update
  7.3 0.8 reduce-window_clone.1
  8.1 0.7 subtract_bitcast_fusion
  9.1 8.8 %broadcast_select_fusion.3 = (bf16[128,127,128]{2,0,1:T(8,128)(2,1)}, bf16[128,127,128]{2,0,1:T(8,128)(2,1)}) fusion(pred[128,127]{0,1:T(8,128)(4,1)S(1)} %get-tuple-element.30, pred[128,127]{0,1:T(8,128)(4,1)S(1)} %get-tuple-element.31, bf16[128,128]{1,0:T(8,128)(2,1)S(1)} %copy-done, s32[128,127]{0,1:T(8,128)S(1)} %iota_subtract_fusion), kind=kOutput, calls=%fused_computation.16 | convolution fusion | flops 540999680 | bytes 8453376 | tf_op jit(solution)/shard_map/ijt,tg->ijg/dot_general | solution.py:35
  17.9 10.4 %broadcast_select_fusion.1 = (bf16[128,128,128]{2,1,0:T(8,128)(2,1)}, bf16[128,128,128]{2,1,0:T(8,128)(2,1)}) fusion(pred[128,128]{1,0:T(8,128)(4,1)S(1)} %get-tuple-element.33, pred[128,128]{1,0:T(8,128)(4,1)S(1)} %get-tuple-element.32, bf16[128,128]{1,0:T(8,128)(2,1)S(1)} %copy-done, s32[128,128]{1,0:T(8,128)S(1)} %iota_subtract_fusion.1), kind=kOutput, calls=%fused_computation.13 | convolution fusion | flops 545259520 | bytes 8519680 | tf_op jit(solution)/shard_map/ijt,tg->ijg/dot_general | solution.py:35
  28.4 153.1 %all-gather.2.cloned.1.call-done = bf16[2048,6144]{1,0:T(8,128)(2,1)} async-done(((bf16[2048,384]{1,0:T(8,128)(2,1)}), bf16[2048,6144]{1,0:T(8,128)(2,1)}) %all-gather.2.cloned.1.call-update) | async-done | bytes 25165840 | tf_op jit(solution)/shard_map/all_gather | solution.py:46
  181.5 11.9 %convolution_convert_fusion = bf16[256,6144]{1,0:T(8,128)(2,1)S(1)} fusion(bf16[256,2048]{1,0:T(8,128)(2,1)} %param.6, bf16[2048,6144]{1,0:T(8,128)(2,1)} %all-gather.2.cloned.1.call-done), kind=kOutput, calls=%fused_computation.9 | convolution fusion | flops 6444023808 | bytes 29360128 | tf_op jit(solution)/shard_map/dot_general | solution.py:44
  193.4 4.6 %collective-permute-start = (bf16[6,6144]{1,0:T(8,128)(2,1)S(1)}, bf16[6,6144]{1,0:T(8,128)(2,1)S(1)}, u32[]{:S(2)}, u32[]{:S(2)}) collective-permute-start(bf16[6,6144]{1,0:T(8,128)(2,1)S(1)} %slice.92), channel_id=1, source_target_pairs={{0,1},{1,2},{2,3},{3,4},{4,5},{5,6},{6,7},{7,8},{8,9},{9,10},{10,1... | collective-permute-start | bytes 221192 | tf_op jit(solution)/shard_map/ppermute | solution.py:10
  198.1 6.7 %copy.32 = bf16[128,128,128]{1,0,2:T(8,128)(2,1)} copy(bf16[128,128,128]{2,1,0:T(8,128)(2,1)} %get-tuple-element.8) | data formatting | bytes 8388608 | tf_op jit(solution)/shard_map/jit(_where)/select_n | solution.py:73
  204.7 7.2 %copy.34 = bf16[128,127,128]{1,0,2:T(8,128)(2,1)} copy(bf16[128,127,128]{2,0,1:T(8,128)(2,1)} %get-tuple-element.10) | data formatting | bytes 8323072 | tf_op jit(solution)/shard_map/jit(_where)/select_n | solution.py:74
  211.9 6.7 %copy.28 = bf16[128,128,128]{1,0,2:T(8,128)(2,1)} copy(bf16[128,128,128]{2,1,0:T(8,128)(2,1)} %get-tuple-element.7) | data formatting | bytes 8388608 | tf_op jit(solution)/shard_map/jit(_where)/select_n | solution.py:73
  218.6 7.2 %copy.30 = bf16[128,127,128]{1,0,2:T(8,128)(2,1)} copy(bf16[128,127,128]{2,0,1:T(8,128)(2,1)} %get-tuple-element.9) | data formatting | bytes 8323072 | tf_op jit(solution)/shard_map/jit(_where)/select_n | solution.py:74
  225.8 9.8 %multiply_add_fusion = f32[256,6144]{1,0:T(8,128)S(1)} fusion(bf16[256,6144]{1,0:T(8,128)(2,1)S(1)} %convolution_convert_fusion, bf16[6,6144]{1,0:T(8,128)(2,1)S(1)} %collective-permute-done, f32[6144]{0:T(1024)S(1)} %bitcast.52, f32[6144]{0:T(1024)S(1)} %bitcast.53, f32[6144]{0:T(1024)S(1)} %bitcast.48, f32[6144]{0:T(1024)S(1)} %bitcast.49, ...), kind=kLoop, calls=%fused_computation.10 | loop fusion | flops 70778880 | bytes 9684736 | tf_op jit(solution)/shard_map/add | solution.py:26
  235.7 2.6 copy-done.2
  238.6 1.1 fusion.24
  240.3 2.4 collective-permute-start.1
  242.6 4.5 %fusion.29 = f32[128,16,128]{2,1,0:T(8,128)S(1)} fusion(bf16[128,128,16]{0,2,1:T(8,128)(2,1)S(1)} %bitcast.44, bf16[128,128,128]{1,0,2:T(8,128)(2,1)} %copy.32), kind=kOutput, calls=%fused_computation.62 | convolution fusion | flops 67108864 | bytes 5767168 | tf_op jit(solution)/shard_map/ijg,jgc->igc/dot_general | solution.py:81
  247.1 2.3 convolution_add_fusion.1
  249.4 1.4 copy.36
  251.0 4.5 %fusion.28 = f32[128,16,128]{2,1,0:T(8,128)S(1)} fusion(bf16[128,128,16]{0,2,1:T(8,128)(2,1)S(1)} %bitcast.46, bf16[128,128,128]{1,0,2:T(8,128)(2,1)} %copy.28), kind=kOutput, calls=%fused_computation.61 | convolution fusion | flops 67108864 | bytes 5767168 | tf_op jit(solution)/shard_map/ijg,jgc->igc/dot_general | solution.py:81
  255.5 0.3 copy.29
  255.8 4.4 %convolution_add_fusion.2 = f32[128,16,128]{2,1,0:T(8,128)S(1)} fusion(f32[128,16,128]{2,1,0:T(8,128)S(1)} %fusion.28, bf16[127,128,16]{0,2,1:T(8,128)(2,1)S(1)} %bitcast.45, bf16[128,127,128]{1,0,2:T(8,128)(2,1)} %copy.30), kind=kOutput, calls=%fused_computation.35 | convolution fusion | flops 66846720 | bytes 6778880 | tf_op jit(solution)/shard_map/ijg,jgc->igc/dot_general | solution.py:84
  260.2 0.4 copy.35
  260.6 7.9 %fusion.11 = bf16[256,2048]{1,0:T(8,128)(2,1)} fusion(bf16[2048,2048]{1,0:T(8,128)(2,1)} %param.11, bf16[256,2048]{1,0:T(8,128)(2,1)} %param.6, f32[256,6144]{1,0:T(8,128)} %copy-done.2, f32[128,2048]{1,0:T(8,128)} %copy.36, f32[128,2048]{1,0:T(8,128)S(1)} %copy.35), kind=kOutput, calls=%fused_computation.29 | convolution fusion | flops 2150629376 | bytes 14680064 | tf_op jit(solution)/shard_map/dot_general | solution.py:90
  (29 shorter events, 1.6 us)
Async XLA Ops:
  6.5 2.5 copy-start
  6.5 175.0 %all-gather.2.cloned.1.call-start = ((), (), s32[]{:S(2)}) async-start(), calls=%async_computation | async-start | bytes 26738688 | tf_op jit(solution)/shard_map/all_gather | solution.py:46
  17.9 10.4 %copy-start.4 = (f32[7,6144]{1,0:T(8,128)S(1)}, f32[7,6144]{1,0:T(8,128)}, u32[]{:S(2)}) copy-start(f32[7,6144]{1,0:T(8,128)} %param.9) | copy-start | bytes 516100
  193.4 32.4 %collective-permute-start = (bf16[6,6144]{1,0:T(8,128)(2,1)S(1)}, bf16[6,6144]{1,0:T(8,128)(2,1)S(1)}, u32[]{:S(2)}, u32[]{:S(2)}) collective-permute-start(bf16[6,6144]{1,0:T(8,128)(2,1)S(1)} %slice.92), channel_id=1, source_target_pairs={{0,1},{1,2},{2,3},{3,4},{4,5},{5,6},{6,7},{7,8},{8,9},{9,10},{10,1... | collective-permute-start | bytes 221192 | tf_op jit(solution)/shard_map/ppermute | solution.py:10
  235.7 2.6 copy-start.2
  240.3 6.8 %copy-start.3 = (bf16[128,127,128]{1,0,2:T(8,128)(2,1)S(1)}, bf16[128,127,128]{1,0,2:T(8,128)(2,1)}, u32[]{:S(2)}) copy-start(bf16[128,127,128]{1,0,2:T(8,128)(2,1)} %copy.34) | copy-start | bytes 12484612
  240.3 15.2 %collective-permute-start.1 = (bf16[127,2048]{1,0:T(8,128)(2,1)}, bf16[127,2048]{1,0:T(8,128)(2,1)S(1)}, u32[]{:S(2)}, u32[]{:S(2)}) collective-permute-start(bf16[127,2048]{1,0:T(8,128)(2,1)} %get-tuple-element.11), channel_id=1, source_target_pairs={{0,1},{1,2},{2,3},{3,4},{4,5},{5,6},{6,7},{7,8},{8,9},{9,10},{10,1... | collective-permute-start | bytes 1560584 | tf_op jit(solution)/shard_map/ppermute | solution.py:10
  260.6 7.9 %copy-start.1 = (bf16[128,128]{1,0:T(8,128)(2,1)S(1)}, bf16[128,128]{1,0:T(8,128)(2,1)}, u32[]{:S(2)}) copy-start(bf16[128,128]{1,0:T(8,128)(2,1)} %param.10) | copy-start | bytes 98308
Sparse Core Ops, SparseCore 0:
  9.8 171.6 all-gather.1
where the time goes:
time: 276 us; the launch traced here: 275 us
  waiting for transfers between devices  154 us (56%)
  matrix products  54.6 us (20%)
  local copies, waits for them, and re-layouts  34.5 us (12%)
  between operations  13.6 us (5%)
  other arithmetic  11.8 us (4%)
  starting transfers between devices  6.97 us (3%)
    all_gather x1, waiting for transfers between devices, local(): lax.all_gather(in_weight, 'fsdp', axis=1, tiled=True)  153 us
    dot_general x2, matrix products, tap_table(): jnp.einsum('ijt,tg->ijg', one_hot, long_filter, preferred_element_type=jn...  19.2 us
    select_n x2, local copies, waits for them, and re-layouts, local(): jnp.where((prev_tap <= block_pos[:, None])[:, :, None], prev_table, 0.0)  14.4 us
    select_n x2, local copies, waits for them, and re-layouts, local(): jnp.where((cur_tap <= block_pos[:, None])[:, :, None], cur_table, 0.0)  13.4 us
    dot_general x1, matrix products, local(): jnp.dot(tokens, lax.all_gather(in_weight, 'fsdp', axis=1, tiled=True), pr...  11.9 us
    add x1, other arithmetic, featurize(): total + taps[tap_index] * jnp.where((position >= tap_index)[:, None], par...  9.84 us
    dot_general x2, matrix products, local(): jnp.einsum('ijg,jgc->igc', cur_kernel, cur_src, preferred_element_type=jn...  8.91 us
    dot_general x1, matrix products, local(): jnp.dot(gated_out, out_weight, preferred_element_type=jnp.float32)  7.87 us
  transfers between devices with their start and end apart: 3, of which 1 were waited for; matrix products, arithmetic and copies ran while one was open for 22% of the time, Pallas kernels for 0%

commit v1 on v0

--- a/solution.py
+++ b/solution.py
@@ -43,7 +43,15 @@
     filter_len, group_count = long_filter.shape
     projected = jnp.dot(
         tokens,
-        lax.all_gather(in_weight, "fsdp", axis=1, tiled=True),
+        jnp.concatenate(
+            lax.all_to_all(
+                jnp.stack([in_weight for _ in range(lax.axis_size("fsdp"))]),
+                axis_name="fsdp",
+                split_axis=0,
+                concat_axis=0,
+            ),
+            1,
+        ),
         preferred_element_type=jnp.float32,
     ).astype(jnp.bfloat16)
     lengths_row = seq_lengths[0]

time: 276 us -> 567 us (2.05)
  waiting for transfers between devices: 154 us -> 436 us
  between operations: 13.6 us -> 0.21 us
  local copies, waits for them, and re-layouts: 34.5 us -> 44.9 us
  starting transfers between devices: 6.97 us -> 15.7 us
    all_to_all x0 -> x1, waiting for transfers between devices: none -> 436 us  [local(): lax.all_to_all(jnp.stack([in_weight for _ in range(lax.axis_size('fsdp'))...]
    all_gather x1 -> x0, waiting for transfers between devices: 153 us -> none  [local(): lax.all_gather(in_weight, 'fsdp', axis=1, tiled=True)]
    another operation x0 -> x1, local copies, waits for them, and re-layouts: none -> 8.64 us  [local(): jnp.stack([in_weight for _ in range(lax.axis_size('fsdp'))])]
    all_to_all x0 -> x1, starting transfers between devices: none -> 7.76 us  [local(): lax.all_to_all(jnp.stack([in_weight for _ in range(lax.axis_size('fsdp'))...]
  transfers between devices with their start and end apart: 3 -> 3, of which waited for: 1 -> 1; matrix products, arithmetic and copies ran while one was open for 22% -> 11% of each run, Pallas kernels for 0% -> 0%
where the time goes in v1:
time: 567 us; the launch traced here: 562 us
  waiting for transfers between devices  436 us (77%)
  matrix products  54.7 us (10%)
  local copies, waits for them, and re-layouts  44.9 us (8%)
  starting transfers between devices  15.7 us (3%)
  other arithmetic  10.5 us (2%)
    all_to_all x1, waiting for transfers between devices, local(): lax.all_to_all(jnp.stack([in_weight for _ in range(lax.axis_size('fsdp'))...  436 us
    dot_general x2, matrix products, tap_table(): jnp.einsum('ijt,tg->ijg', one_hot, long_filter, preferred_element_type=jn...  19.3 us
    select_n x2, local copies, waits for them, and re-layouts, local(): jnp.where((prev_tap <= block_pos[:, None])[:, :, None], prev_table, 0.0)  14.4 us
    select_n x2, local copies, waits for them, and re-layouts, local(): jnp.where((cur_tap <= block_pos[:, None])[:, :, None], cur_table, 0.0)  13.4 us
    dot_general x1, matrix products, local(): jnp.dot(tokens, jnp.concatenate(lax.all_to_all(jnp.stack([in_weight for _...  11.9 us
  transfers between devices with their start and end apart: 3, of which 1 were waited for; matrix products, arithmetic and copies ran while one was open for 11% of the time, Pallas kernels for 0%

profile of v1, /device:TPU:1, one launch (start us, length us, event | category | flops | bytes accessed | tf_op | source)
XLA Modules:
  0.0 562.3 jit_solution(13287580985086296765)
XLA Ops:
  0.0 1.7 copy.28
  1.7 8.6 %stack.2 = bf16[16,2048,384]{1,2,0:T(8,128)(2,1)} broadcast(bf16[2048,384]{0,1:T(8,128)(2,1)S(1)} %copy.28), dimensions={1,2} | broadcast | bytes 26738688 | tf_op jit(solution)/shard_map/stack | solution.py:48
  10.4 7.8 %all-to-all-start = ((bf16[16,2048,384]{1,2,0:T(8,128)(2,1)}), bf16[16,2048,384]{1,2,0:T(8,128)(2,1)}, u32[]{:S(2)}, u32[]{:S(2)}) async-start(bf16[16,2048,384]{1,2,0:T(8,128)(2,1)} %stack.2), calls=%async_computation | async-start | bytes 50331648 | tf_op jit(solution)/shard_map/all_to_all | solution.py:47
  18.6 8.9 %broadcast_select_fusion.3 = (bf16[128,127,128]{2,0,1:T(8,128)(2,1)}, bf16[128,127,128]{2,0,1:T(8,128)(2,1)}) fusion(pred[128,127]{0,1:T(8,128)(4,1)S(1)} %get-tuple-element.30, pred[128,127]{0,1:T(8,128)(4,1)S(1)} %get-tuple-element.31, bf16[128,128]{1,0:T(8,128)(2,1)S(1)} %copy-done, s32[128,127]{0,1:T(8,128)S(1)} %iota_subtract_fusion), kind=kOutput, calls=%fused_computation.16 | convolution fusion | flops 540999680 | bytes 8453376 | tf_op jit(solution)/shard_map/ijt,tg->ijg/dot_general | solution.py:35
  27.5 10.4 %broadcast_select_fusion.1 = (bf16[128,128,128]{2,1,0:T(8,128)(2,1)}, bf16[128,128,128]{2,1,0:T(8,128)(2,1)}) fusion(pred[128,128]{1,0:T(8,128)(4,1)S(1)} %get-tuple-element.33, pred[128,128]{1,0:T(8,128)(4,1)S(1)} %get-tuple-element.32, bf16[128,128]{1,0:T(8,128)(2,1)S(1)} %copy-done, s32[128,128]{1,0:T(8,128)S(1)} %iota_subtract_fusion.1), kind=kOutput, calls=%fused_computation.13 | convolution fusion | flops 545259520 | bytes 8519680 | tf_op jit(solution)/shard_map/ijt,tg->ijg/dot_general | solution.py:35
  38.0 436.2 %all-to-all-done = bf16[16,2048,384]{1,2,0:T(8,128)(2,1)} async-done(((bf16[16,2048,384]{1,2,0:T(8,128)(2,1)}), bf16[16,2048,384]{1,2,0:T(8,128)(2,1)}, u32[]{:S(2)}, u32[]{:S(2)}) %all-to-all-start) | async-done | bytes 25165856 | tf_op jit(solution)/shard_map/all_to_all | solution.py:47
  474.2 11.9 %convolution_convert_fusion = bf16[256,6144]{1,0:T(8,128)(2,1)S(1)} fusion(bf16[256,2048]{1,0:T(8,128)(2,1)} %param.6, bf16[2048,6144]{0,1:T(8,128)(2,1)} %bitcast.3), kind=kOutput, calls=%fused_computation.9 | convolution fusion | flops 6444023808 | bytes 29360128 | tf_op jit(solution)/shard_map/dot_general | solution.py:44
  486.2 5.6 collective-permute-start
  491.8 6.7 %copy.34 = bf16[128,128,128]{1,0,2:T(8,128)(2,1)} copy(bf16[128,128,128]{2,1,0:T(8,128)(2,1)} %get-tuple-element.8) | data formatting | bytes 8388608 | tf_op jit(solution)/shard_map/jit(_where)/select_n | solution.py:81
  498.5 7.2 %copy.36 = bf16[128,127,128]{1,0,2:T(8,128)(2,1)} copy(bf16[128,127,128]{2,0,1:T(8,128)(2,1)} %get-tuple-element.10) | data formatting | bytes 8323072 | tf_op jit(solution)/shard_map/jit(_where)/select_n | solution.py:82
  505.7 6.7 %copy.30 = bf16[128,128,128]{1,0,2:T(8,128)(2,1)} copy(bf16[128,128,128]{2,1,0:T(8,128)(2,1)} %get-tuple-element.7) | data formatting | bytes 8388608 | tf_op jit(solution)/shard_map/jit(_where)/select_n | solution.py:81
  512.4 7.2 %copy.32 = bf16[128,127,128]{1,0,2:T(8,128)(2,1)} copy(bf16[128,127,128]{2,0,1:T(8,128)(2,1)} %get-tuple-element.9) | data formatting | bytes 8323072 | tf_op jit(solution)/shard_map/jit(_where)/select_n | solution.py:82
  519.6 9.8 %multiply_add_fusion = f32[256,6144]{1,0:T(8,128)S(1)} fusion(bf16[256,6144]{1,0:T(8,128)(2,1)S(1)} %convolution_convert_fusion, bf16[6,6144]{1,0:T(8,128)(2,1)S(1)} %collective-permute-done, f32[6144]{0:T(1024)S(1)} %bitcast.55, f32[6144]{0:T(1024)S(1)} %bitcast.56, f32[6144]{0:T(1024)S(1)} %bitcast.51, f32[6144]{0:T(1024)S(1)} %bitcast.52, ...), kind=kLoop, calls=%fused_computation.10 | loop fusion | flops 70778880 | bytes 9684736 | tf_op jit(solution)/shard_map/add | solution.py:26
  529.4 2.6 copy-done.2
  532.4 1.1 fusion.24
  534.0 2.4 collective-permute-start.1
  536.4 4.5 fusion.29
  540.9 2.3 convolution_add_fusion.1
  543.2 1.4 copy.38
  544.8 4.5 fusion.28
  549.3 0.3 copy.31
  549.6 4.4 convolution_add_fusion.2
  554.0 0.4 copy.37
  554.4 7.9 %fusion.11 = bf16[256,2048]{1,0:T(8,128)(2,1)} fusion(bf16[2048,2048]{1,0:T(8,128)(2,1)} %param.11, bf16[256,2048]{1,0:T(8,128)(2,1)} %param.6, f32[256,6144]{1,0:T(8,128)} %copy-done.2, f32[128,2048]{1,0:T(8,128)} %copy.38, f32[128,2048]{1,0:T(8,128)S(1)} %copy.37), kind=kOutput, calls=%fused_computation.29 | convolution fusion | flops 2150629376 | bytes 14680064 | tf_op jit(solution)/shard_map/dot_general | solution.py:98
  (32 shorter events, 1.8 us)
Async XLA Ops:
  0.0 18.6 %copy-start = (bf16[128,128]{1,0:T(8,128)(2,1)S(1)}, bf16[128,128]{1,0:T(8,128)(2,1)}, u32[]{:S(2)}) copy-start(bf16[128,128]{1,0:T(8,128)(2,1)} %param.10) | copy-start | bytes 98308
  10.4 7.8 %copy-start.5 = (s32[1,4]{1,0:T(1,128)S(1)}, s32[1,4]{1,0:T(1,128)}, u32[]{:S(2)}) copy-start(s32[1,4]{1,0:T(1,128)} %param.7) | copy-start | bytes 52
  10.4 463.9 %all-to-all-start = ((bf16[16,2048,384]{1,2,0:T(8,128)(2,1)}), bf16[16,2048,384]{1,2,0:T(8,128)(2,1)}, u32[]{:S(2)}, u32[]{:S(2)}) async-start(bf16[16,2048,384]{1,2,0:T(8,128)(2,1)} %stack.2), calls=%async_computation | async-start | bytes 50331648 | tf_op jit(solution)/shard_map/all_to_all | solution.py:47
  27.5 10.4 %copy-start.4 = (f32[7,6144]{1,0:T(8,128)S(1)}, f32[7,6144]{1,0:T(8,128)}, u32[]{:S(2)}) copy-start(f32[7,6144]{1,0:T(8,128)} %param.9) | copy-start | bytes 516100
  486.2 33.4 %collective-permute-start = (bf16[6,6144]{1,0:T(8,128)(2,1)S(1)}, bf16[6,6144]{1,0:T(8,128)(2,1)S(1)}, u32[]{:S(2)}, u32[]{:S(2)}) collective-permute-start(bf16[6,6144]{1,0:T(8,128)(2,1)S(1)} %slice.92), channel_id=1, source_target_pairs={{0,1},{1,2},{2,3},{3,4},{4,5},{5,6},{6,7},{7,8},{8,9},{9,10},{10,1... | collective-permute-start | bytes 221192 | tf_op jit(solution)/shard_map/ppermute | solution.py:10
  529.4 2.6 copy-start.2
  534.0 6.8 %copy-start.3 = (bf16[128,127,128]{1,0,2:T(8,128)(2,1)S(1)}, bf16[128,127,128]{1,0,2:T(8,128)(2,1)}, u32[]{:S(2)}) copy-start(bf16[128,127,128]{1,0,2:T(8,128)(2,1)} %copy.36) | copy-start | bytes 12484612
  534.0 15.2 %collective-permute-start.1 = (bf16[127,2048]{1,0:T(8,128)(2,1)}, bf16[127,2048]{1,0:T(8,128)(2,1)S(1)}, u32[]{:S(2)}, u32[]{:S(2)}) collective-permute-start(bf16[127,2048]{1,0:T(8,128)(2,1)} %get-tuple-element.11), channel_id=1, source_target_pairs={{0,1},{1,2},{2,3},{3,4},{4,5},{5,6},{6,7},{7,8},{8,9},{9,10},{10,1... | collective-permute-start | bytes 1560584 | tf_op jit(solution)/shard_map/ppermute | solution.py:10
  554.4 7.9 %copy-start.1 = (bf16[128,128]{1,0:T(8,128)(2,1)S(1)}, bf16[128,128]{1,0:T(8,128)(2,1)}, u32[]{:S(2)}) copy-start(bf16[128,128]{1,0:T(8,128)(2,1)} %param.10) | copy-start | bytes 98308
